TPU v7x, 32 devices: a whole 2x2x4 slice. The times are simulated.
32 devices in a mesh: seq: 8 (over z, x), ch: 4 (over y, core).
Axes of the slice: x: 2, y: 2, z: 4, core: 2. Of those that a mesh axis runs over, the one named last changes fastest.
Arguments:
- xin: bfloat16 [8192, 16384], P('seq', 'ch'), may hold values from -6 to 6
- gate_in: bfloat16 [8192, 16384], P('seq', 'ch'), may hold values from -6 to 6
- bc_proj: bfloat16 [8192, 256], P('seq', 'ch'), may hold values from -6 to 6
- dt_raw: float32 [8192, 128], P('seq', 'ch'), may hold values from -6 to 6
- dt_bias: float32 [128], P('ch'), may hold values from -1 to 1
- rate: float32 [128], P('ch'), may hold values from 6.1035156e-05 to 0.1
- skip_gain: float32 [128], P('ch'), may hold values from 0.5 to 2
- conv_x: bfloat16 [4, 16384], P(None, 'ch'), may hold values from -3 to 3
- conv_bc: bfloat16 [4, 256], P(None, 'ch'), may hold values from -3 to 3
- norm_gain: float32 [16384], P('ch'), may hold values from 0.5 to 1.5
- valid_blocks: int32 [8], P('seq'), may hold values from 1 to 8, 48 in all
Outputs:
- mixed: bfloat16 [8192, 16384], P('seq', 'ch')
Inputs may be any that keep to these rules, and one draw needn't show every extreme that they name: valid_blocks sums to 48; some entry equals 8.
All inputs are finite; a program needn't handle non-finite values.
Results may differ from a plain program's by a relative error of at most 0.0034.
Values may be sent and summed in bfloat16 or wider, within the bound.
No kernel may reach another device: no remote copies, remote signals or barrier semaphores. Data moves between devices by JAX's collectives and lax.ppermute only.
A program may use at most 256 MiB of HBM per device.

v0:
```python
import jax
import jax.numpy as jnp
from jax import lax
from jax.sharding import PartitionSpec as P

SEGMENT_LENGTH = 256
BLOCK = 128
INNER = 16384


def passed_along(block, axis, distance):
    devices = range(lax.axis_size(axis))
    route = [(i - distance, i) for i in devices if i - distance in devices]
    return lax.ppermute(block, axis, route)


def prefix(part, axis, combine, identity):
    place = lax.axis_index(axis)
    gathered = jax.tree.map(lambda a: lax.all_gather(a, axis), part)
    state = jax.tree.map(lambda a, e: jnp.zeros_like(a) + jnp.asarray(e, a.dtype), part, identity)

    def one(turn, state):
        return combine(
            state, jax.tree.map(lambda a: lax.dynamic_index_in_dim(a, turn, 0, False), gathered)
        )

    return lax.fori_loop(0, place, one, state)


def scan_states(factor, state, axis):
    count = lax.axis_size(axis)
    heads, size, width = state.shape
    piece = size // count
    parts = state.reshape(heads, count, piece, width).transpose(1, 0, 2, 3)
    got = lax.all_to_all(parts, axis, 0, 0, tiled=True)
    decays = lax.all_gather(factor, axis)
    running = jnp.zeros((heads, piece, width), jnp.float32)
    entries = []
    for index in range(count):
        entries.append(running)
        running = decays[index][:, None, None] * running + got[index]
    back = lax.all_to_all(jnp.stack(entries, axis=0), axis, 0, 0, tiled=True)
    return back.transpose(1, 0, 2, 3).reshape(heads, size, width)


def conv_silu(signal, tail_rows, weights):
    stacked = jnp.concatenate([tail_rows, signal], axis=0)
    kernel_taps = weights.shape[0]
    length = signal.shape[0]
    accum = jnp.zeros(signal.shape, jnp.float32)
    for offset in range(kernel_taps):
        accum = accum + weights[offset].astype(jnp.float32) * stacked[
            offset : offset + length
        ].astype(jnp.float32)
    return jax.nn.silu(accum).astype(jnp.bfloat16)


def combine_states(earlier, latter):
    return (earlier[0] * latter[0], latter[0][:, None, None] * earlier[1] + latter[1])


def local(
    xin,
    gate_in,
    bc_proj,
    dt_raw,
    dt_bias,
    rate,
    skip_gain,
    conv_x,
    conv_bc,
    norm_gain,
    valid_blocks,
):
    row_count, channels = xin.shape
    head_count = dt_raw.shape[1]
    head_size = channels // head_count
    span_count = row_count // SEGMENT_LENGTH
    kernel_taps = conv_x.shape[0]
    live_rows = valid_blocks[0] * BLOCK
    tail_x = lax.dynamic_slice_in_dim(xin, live_rows - (kernel_taps - 1), kernel_taps - 1, 0)
    tail_bc = lax.dynamic_slice_in_dim(bc_proj, live_rows - (kernel_taps - 1), kernel_taps - 1, 0)
    prev_x, prev_bc = passed_along((tail_x, tail_bc), "seq", 1)
    xconv = conv_silu(xin, prev_x, conv_x)
    bc_local = conv_silu(bc_proj, prev_bc, conv_bc)
    bc_full = lax.all_gather(bc_local, "ch", axis=1, tiled=True)
    state_size = bc_full.shape[1] // 2
    row_valid = (jnp.arange(row_count) < live_rows).astype(jnp.float32)
    step_size = jax.nn.softplus(dt_raw + dt_bias[None, :]) * row_valid[:, None]
    xfour = xconv.reshape(span_count, SEGMENT_LENGTH, head_count, head_size)
    b_three = bc_full[:, :state_size].reshape(span_count, SEGMENT_LENGTH, state_size)
    c_three = bc_full[:, state_size:].reshape(span_count, SEGMENT_LENGTH, state_size)
    step_three = step_size.reshape(span_count, SEGMENT_LENGTH, head_count)
    cumul = jnp.cumsum(-rate[None, None, :] * step_three, axis=1)
    scores = jnp.einsum("cqn,csn->cqs", c_three, b_three, preferred_element_type=jnp.float32)
    cum_heads = jnp.transpose(cumul, (0, 2, 1))
    diff = cum_heads[:, :, :, None] - cum_heads[:, :, None, :]
    causal = jnp.arange(SEGMENT_LENGTH)[:, None] >= jnp.arange(SEGMENT_LENGTH)[None, :]
    decay = jnp.where(causal, jnp.exp(jnp.where(causal, diff, 0.0)), 0.0)
    weights = (
        scores[:, None] * decay * jnp.transpose(step_three, (0, 2, 1))[:, :, None, :]
    ).astype(jnp.bfloat16)
    intra = jnp.einsum("chqs,cshp->cqhp", weights, xfour, preferred_element_type=jnp.float32)
    last_cum = cum_heads[:, :, -1]
    to_end = jnp.exp(last_cum[:, None, :] - cumul) * step_three
    x_weighted = (xfour.astype(jnp.float32) * to_end[..., None]).astype(jnp.bfloat16)
    block_state = jnp.einsum(
        "csn,cshp->chnp", b_three, x_weighted, preferred_element_type=jnp.float32
    )
    block_decay = jnp.exp(last_cum)
    current = jnp.zeros((head_count, state_size, head_size), jnp.float32)
    factor = jnp.ones((head_count,), jnp.float32)
    local_enter = []
    factor_list = []
    for index in range(span_count):
        local_enter.append(current)
        factor_list.append(factor)
        current = block_decay[index][:, None, None] * current + block_state[index]
        factor = factor * block_decay[index]
    group_state = scan_states(factor, current, "seq")
    state_enter = jnp.stack(
        [
            local_enter[index] + factor_list[index][:, None, None] * group_state
            for index in range(span_count)
        ],
        axis=0,
    )
    inter = jnp.einsum(
        "cqn,chnp->cqhp", c_three.astype(jnp.float32), state_enter, precision=lax.Precision.HIGHEST
    )
    inter = inter * jnp.exp(cumul)[..., None]
    y_full = intra + inter + skip_gain[None, None, :, None] * xfour.astype(jnp.float32)
    y_full = y_full.reshape(row_count, channels)
    gated = y_full * jax.nn.silu(gate_in.astype(jnp.float32))
    square_sum = lax.psum(jnp.sum(gated * gated, axis=1), "ch")
    mean_sq = square_sum / INNER
    normed = gated * lax.rsqrt(mean_sq + 1e-05)[:, None] * norm_gain[None, :] * row_valid[:, None]
    return normed.astype(jnp.bfloat16)


def solution(mesh):
    placed = (
        P("seq", "ch"),
        P("seq", "ch"),
        P("seq", "ch"),
        P("seq", "ch"),
        P("ch"),
        P("ch"),
        P("ch"),
        P(None, "ch"),
        P(None, "ch"),
        P("ch"),
        P("seq"),
    )
    return jax.shard_map(
        local, mesh=mesh, in_specs=placed, out_specs=P("seq", "ch"), check_vma=False
    )
```

profile of v0, /device:TPU:0, one launch (start us, length us, event | category | flops | bytes accessed | tf_op | source)
XLA Modules:
  0.0 295.1 jit_solution(8217255166965492911)
XLA Ops:
  0.7 0.8 constant_dynamic-slice_fusion
  1.5 4.9 %collective-permute-start.1 = (bf16[3,64]{0,1:T(8,128)(2,1)S(1)}, bf16[3,64]{0,1:T(8,128)(2,1)S(1)}, u32[]{:S(2)}, u32[]{:S(2)}) collective-permute-start(bf16[3,64]{0,1:T(8,128)(2,1)S(1)} %constant_dynamic-slice_fusion), channel_id=1, source_target_pairs={{0,4},{4,8},{8,12},{12,16},{16,20},{20,24},{24,28},{1,5},{5,9},{9,... | collective-permute-start | bytes 1160 | tf_op jit(solution)/shard_map/ppermute | solution.py:14
  6.3 0.9 constant_dynamic-slice_fusion.1
  7.2 3.5 %collective-permute-start = (bf16[3,4096]{1,0:T(4,128)(2,1)S(1)}, bf16[3,4096]{1,0:T(4,128)(2,1)S(1)}, u32[]{:S(2)}, u32[]{:S(2)}) collective-permute-start(bf16[3,4096]{1,0:T(4,128)(2,1)S(1)} %constant_dynamic-slice_fusion.1), channel_id=1, source_target_pairs={{0,4},{4,8},{8,12},{12,16},{16,20},{20,24},{24,28},{1,5},{5,9},{9,... | collective-permute-start | bytes 73736 | tf_op jit(solution)/shard_map/ppermute | solution.py:14
  10.7 1.1 fusion.38
  11.7 0.1 reshape.136
  11.8 0.7 neg.21
  12.5 0.1 multiply_bitcast_fusion
  12.6 0.1 reshape.168
  12.7 2.3 reduce-window.6
  15.0 0.1 slice.185
  15.1 0.1 copy.56
  15.3 0.1 copy_bitcast_fusion
  15.4 0.2 slice_reduce_fusion
  15.6 0.1 copy.62
  15.7 0.1 bitcast_multiply_fusion
  15.8 1.0 slice_convert_fusion.3
  16.8 0.8 bitcast_convert_fusion.3
  17.7 0.0 collective-permute-done.1
  17.7 1.5 multiply_convert_fusion.6
  19.2 7.2 %all_gather.7 = bf16[1024,256]{0,1:T(8,128)(2,1)S(1)} all-gather(bf16[1024,64]{0,1:T(8,128)(2,1)S(1)} %multiply_convert_fusion.6), channel_id=1, replica_groups=mesh['seq'=8,'ch'=4] {'ch'}, dimensions={1}, use_global_device_ids=true | all-gather | bytes 655360 | tf_op jit(solution)/shard_map/all_gather | solution.py:86
  26.5 0.2 copy.82
  26.6 0.0 collective-permute-done
  26.6 18.8 %fusion.26 = bf16[128,8,32,128]{3,1,2,0:T(8,128)(2,1)} fusion(bf16[1024,4096]{1,0:T(8,128)(2,1)} %param.11, f32[4096]{0:T(1024)S(1)} %bitcast.133, bf16[3,4096]{1,0:T(4,128)(2,1)S(1)} %collective-permute-done, f32[4096]{0:T(1024)S(1)} %bitcast.134, f32[4096]{0:T(1024)S(1)} %bitcast.132, f32[4096]{0:T(1024)S(1)} %bitcast.131), kind=kLoop, calls=%fused_computation.37 | loop fusion | flops 104857600 | bytes 16867328
  45.5 9.4 %copy.84 = bf16[128,8,32,128]{3,2,1,0:T(8,128)(2,1)} copy(bf16[128,8,32,128]{3,1,2,0:T(8,128)(2,1)} %fusion.26) | data formatting | bytes 16777216
  54.9 13.7 %copy.60 = bf16[4,256,32,128]{1,3,2,0:T(8,128)(2,1)} copy(bf16[4,256,32,128]{3,2,1,0:T(8,128)(2,1)} %bitcast.118) | data formatting | bytes 16777216 | tf_op jit(solution)/shard_map/reshape | solution.py:90
  68.6 6.3 %fusion.27 = f32[4,32,128,128]{3,2,1,0:T(8,128)S(1)} fusion(bf16[4,256,128,1]{2,1,3,0:T(8,128)(2,1)S(1)} %bitcast.126, bf16[4,256,32,128]{1,3,2,0:T(8,128)(2,1)} %copy.60, f32[4,256,32]{1,2,0:T(8,128)S(1)} %copy.64), kind=kOutput, calls=%fused_computation.38 | convolution fusion | flops 1086324736 | bytes 17170432 | tf_op jit(solution)/shard_map/csn,cshp->chnp/dot_general | solution.py:107
  74.9 0.0 copy-start
  74.9 0.6 fusion.51
  75.5 2.6 copy-done
  78.1 2.0 fusion.30
  80.2 4.8 %all-to-all-start = ((f32[8,32,16,128]{3,2,1,0:T(8,128)}), f32[8,32,16,128]{3,2,1,0:T(8,128)S(1)}, u32[]{:S(2)}, u32[]{:S(2)}) async-start(f32[8,32,16,128]{3,2,1,0:T(8,128)} %fusion.30), calls=%async_computation | async-start | bytes 4194304 | tf_op jit(solution)/shard_map/all_to_all | solution.py:35
  85.0 50.3 %all-gather = f32[8,1,32]{2,1,0:T(1,128)S(1)} all-gather(f32[1,1,32]{2,1,0:T(1,128)S(1)} %get-tuple-element.35), channel_id=1, replica_groups=mesh['seq'=8,'ch'=4] {'seq'}, dimensions={0}, use_global_device_ids=true | all-gather | bytes 1152 | tf_op jit(solution)/shard_map/all_gather | solution.py:36
  135.2 0.8 broadcast_dynamic-update-slice_fusion
  136.0 0.0 all-to-all-done
  136.0 0.8 fusion.35
  136.8 0.9 constant_dynamic-update-slice_fusion.2
  137.7 0.8 fusion.40
  138.5 0.8 constant_dynamic-update-slice_fusion.1
  139.3 0.8 fusion.41
  140.2 0.8 constant_dynamic-update-slice_fusion
  141.0 0.8 fusion.34
  141.8 10.2 %all-to-all-start.1 = ((f32[8,32,16,128]{3,2,1,0:T(8,128)}), f32[8,32,16,128]{3,2,1,0:T(8,128)S(1)}, u32[]{:S(2)}, u32[]{:S(2)}) async-start(f32[8,32,16,128]{3,2,1,0:T(8,128)} %fusion.34), calls=%async_computation.1 | async-start | bytes 4194304 | tf_op jit(solution)/shard_map/all_to_all | solution.py:42
  152.1 0.1 exponential_bitcast_fusion
  152.2 0.2 copy.52
  152.4 1.3 fusion.53
  153.7 44.1 %all-to-all-done.1 = f32[8,32,16,128]{3,2,1,0:T(8,128)S(1)} async-done(((f32[8,32,16,128]{3,2,1,0:T(8,128)}), f32[8,32,16,128]{3,2,1,0:T(8,128)S(1)}, u32[]{:S(2)}, u32[]{:S(2)}) %all-to-all-start.1) | async-done | bytes 2097184 | tf_op jit(solution)/shard_map/all_to_all | solution.py:42
  197.8 0.3 copy.71
  198.1 0.0 slice-start
  198.1 3.5 %multiply_add_fusion.1 = (f32[1,32,128,128]{3,2,1,0:T(8,128)S(1)}, f32[1,32,128,128]{3,2,1,0:T(8,128)S(1)}, f32[1,32,128,128]{3,2,1,0:T(8,128)S(1)}) fusion(f32[1,32,128,128]{3,2,1,0:T(8,128)S(1)} %bitcast.119, f32[32]{0:T(128)S(1)} %get-tuple-element.6, f32[4,32,128,128]{3,2,1,0:T(8,128)} %copy-done, f32[32]{0:T(128)S(1)} %get-tuple-element.38, ...), kind=kLoop, calls=%fused_computation.48 | loop fusion | flops 5767168 | bytes 14680832 | tf_op jit(solution)/shard_map/add | solution.py:123
  201.6 0.0 slice-start.1
  201.7 0.0 copy-start.1
  201.7 0.0 copy-start.3
  201.7 10.9 %fusion.17 = f32[4,256,32,128]{1,3,2,0:T(8,128)} fusion(bf16[4,256,128,1]{2,1,3,0:T(8,128)(2,1)S(1)} %bitcast.129, f32[1,32,128,128]{3,2,1,0:T(8,128)S(1)} %get-tuple-element.14, f32[1,32,128,128]{3,2,1,0:T(8,128)S(1)} %get-tuple-element.13, f32[1,32,128,128]{3,2,1,0:T(8,128)S(1)} %get-tuple-element.15, f32[1,32,128,128]{3,2,1,0:T(8,128)S(1)} %bitcast.120), kind=kOutput, calls=%fused_computation.28 | convolution fusion | flops 6448742400 | bytes 25427968 | tf_op jit(solution)/shard_map/cqn,chnp->cqhp/dot_general | solution.py:128
  212.6 0.0 slice-done
  212.6 0.0 slice-done.1
  212.6 0.0 copy-done.1
  212.6 0.0 copy-done.3
  212.6 16.9 %fusion.2 = f32[4,256,32,128]{1,3,2,0:T(8,128)} fusion(bf16[4,256,32,128]{1,3,2,0:T(8,128)(2,1)S(1)} %bitcast.117, f32[4,256,32,128]{1,3,2,0:T(8,128)} %fusion.17, f32[4,32,256]{2,1,0:T(8,128)S(1)} %copy.59, f32[4,32,256]{2,1,0:T(8,128)S(1)} %copy_bitcast_fusion, f32[4,256,256]{2,1,0:T(8,128)S(1)} %copy-done.1, pred[256,256]{1,0:T(8,128)(4,1)S(1)} %iota_compare_fusion, ...), kind=kOutput, calls=%fused_computation.7 | convolution fusion | flops 2218786816 | bytes 43450496 | tf_op jit(solution)/shard_map/chqs,cshp->cqhp/dot_general | solution.py:103
  229.6 19.9 %copy.73 = f32[4,256,32,128]{3,2,1,0:T(8,128)} copy(f32[4,256,32,128]{1,3,2,0:T(8,128)} %fusion.2) | data formatting | bytes 33554432 | tf_op jit(solution)/shard_map/add | solution.py:132
  249.4 16.2 %multiply_reduce_fusion = f32[1024]{0:T(1024)S(1)} fusion(bf16[1024,4096]{1,0:T(8,128)(2,1)} %param.12, f32[128,8,32,128]{3,2,1,0:T(8,128)} %bitcast.114), kind=kLoop, calls=%fused_computation.14 | loop fusion | flops 33553408 | bytes 25169920 | tf_op jit(solution)/shard_map/reduce_sum | solution.py:135
  265.6 5.7 %psum.7 = f32[1024]{0:T(1024)S(1)} all-reduce(f32[1024]{0:T(1024)S(1)} %multiply_reduce_fusion), channel_id=1, replica_groups=mesh['seq'=8,'ch'=4] {'ch'}, use_global_device_ids=true, to_apply=%region_3.4 | all-reduce | flops 1024 | bytes 8192 | tf_op jit(solution)/shard_map/psum | solution.py:135
  271.3 0.0 copy-done.2
  271.3 23.8 %multiply_convert_fusion.2 = bf16[1024,4096]{1,0:T(8,128)(2,1)} fusion(f32[1024]{0:T(1024)S(1)} %fusion.44, f32[4096]{0:T(1024)S(1)} %copy-done.2, f32[1024]{0:T(1024)S(1)} %add_rsqrt_fusion, bf16[1024,4096]{1,0:T(8,128)(2,1)} %param.12, f32[128,8,32,128]{3,2,1,0:T(8,128)} %bitcast.115), kind=kLoop, calls=%fused_computation.13 | loop fusion | flops 41943040 | bytes 33579008 | tf_op jit(solution)/shard_map/convert_element_type | solution.py:138
  (16 shorter events, 0.2 us)
Async XLA Ops:
  1.5 16.2 %collective-permute-start.1 = (bf16[3,64]{0,1:T(8,128)(2,1)S(1)}, bf16[3,64]{0,1:T(8,128)(2,1)S(1)}, u32[]{:S(2)}, u32[]{:S(2)}) collective-permute-start(bf16[3,64]{0,1:T(8,128)(2,1)S(1)} %constant_dynamic-slice_fusion), channel_id=1, source_target_pairs={{0,4},{4,8},{8,12},{12,16},{16,20},{20,24},{24,28},{1,5},{5,9},{9,... | collective-permute-start | bytes 1160 | tf_op jit(solution)/shard_map/ppermute | solution.py:14
  7.2 19.4 %collective-permute-start = (bf16[3,4096]{1,0:T(4,128)(2,1)S(1)}, bf16[3,4096]{1,0:T(4,128)(2,1)S(1)}, u32[]{:S(2)}, u32[]{:S(2)}) collective-permute-start(bf16[3,4096]{1,0:T(4,128)(2,1)S(1)} %constant_dynamic-slice_fusion.1), channel_id=1, source_target_pairs={{0,4},{4,8},{8,12},{12,16},{16,20},{20,24},{24,28},{1,5},{5,9},{9,... | collective-permute-start | bytes 73736 | tf_op jit(solution)/shard_map/ppermute | solution.py:14
  74.9 3.2 %copy-start = (f32[4,32,128,128]{3,2,1,0:T(8,128)}, f32[4,32,128,128]{3,2,1,0:T(8,128)S(1)}, u32[]{:S(2)}) copy-start(f32[4,32,128,128]{3,2,1,0:T(8,128)S(1)} %fusion.27) | copy-start | bytes 25165828
  80.2 55.9 %all-to-all-start = ((f32[8,32,16,128]{3,2,1,0:T(8,128)}), f32[8,32,16,128]{3,2,1,0:T(8,128)S(1)}, u32[]{:S(2)}, u32[]{:S(2)}) async-start(f32[8,32,16,128]{3,2,1,0:T(8,128)} %fusion.30), calls=%async_computation | async-start | bytes 4194304 | tf_op jit(solution)/shard_map/all_to_all | solution.py:35
  141.8 56.0 %all-to-all-start.1 = ((f32[8,32,16,128]{3,2,1,0:T(8,128)}), f32[8,32,16,128]{3,2,1,0:T(8,128)S(1)}, u32[]{:S(2)}, u32[]{:S(2)}) async-start(f32[8,32,16,128]{3,2,1,0:T(8,128)} %fusion.34), calls=%async_computation.1 | async-start | bytes 4194304 | tf_op jit(solution)/shard_map/all_to_all | solution.py:42
  198.1 14.5 %slice-start = ((s8[8388608]{0:T(1024)(128)(4,1)}), s8[4194304]{0:T(1024)(128)(4,1)S(1)}, s32[]{:S(2)}) async-start(s8[8388608]{0:T(1024)(128)(4,1)} %bitcast.116), calls=%async_computation.2 | async-start | bytes 8388608
  201.6 11.0 %slice-start.1 = ((s8[8388608]{0:T(1024)(128)(4,1)}), s8[4194304]{0:T(1024)(128)(4,1)S(1)}, s32[]{:S(2)}) async-start(s8[8388608]{0:T(1024)(128)(4,1)} %bitcast.116), calls=%async_computation.3 | async-start | bytes 8388608
  201.7 11.0 %copy-start.1 = (f32[4,256,256]{2,1,0:T(8,128)S(1)}, f32[4,256,256]{2,1,0:T(8,128)}, u32[]{:S(2)}) copy-start(f32[4,256,256]{2,1,0:T(8,128)} %fusion.53) | copy-start | bytes 3145732
  201.7 11.0 %copy-start.3 = (f32[32]{0:T(128)S(1)}, f32[32]{0:T(128)}, u32[]{:S(2)}) copy-start(f32[32]{0:T(128)} %param.17) | copy-start | bytes 388
  249.4 21.9 %copy-start.2 = (f32[4096]{0:T(1024)S(1)}, f32[4096]{0:T(1024)}, u32[]{:S(2)}) copy-start(f32[4096]{0:T(1024)} %param.20) | copy-start | bytes 49156
where the time goes:
time: 296 us; the launch traced here: 295 us
  other arithmetic  78.1 us (26%)
  blocking collectives  63.2 us (21%)
  local copies, waits for them, and re-layouts  50 us (17%)
  waiting for transfers between devices  44.1 us (15%)
  matrix products  35.5 us (12%)
  starting transfers between devices  23.3 us (8%)
    all_gather x1, blocking collectives, scan_states(): decays = lax.all_gather(factor, axis)  50.3 us
    all_to_all x1, waiting for transfers between devices, scan_states(): back = lax.all_to_all(jnp.stack(entries, axis=0), axis, 0, 0, tiled=True)  44.1 us
    unnamed x8, other arithmetic  23.8 us
    convert_element_type x1, other arithmetic, local(): return normed.astype(jnp.bfloat16)  23.8 us
    add x1, local copies, waits for them, and re-layouts, local(): intra + inter + skip_gain[None, None, :, None] * xfour.astype(jnp.float32)  19.9 us
    dot_general x1, matrix products, local(): jnp.einsum('chqs,cshp->cqhp', weights, xfour, preferred_element_type=jnp....  16.9 us
    reduce_sum x1, other arithmetic, local(): square_sum = lax.psum(jnp.sum(gated * gated, axis=1), 'ch')  16.2 us
    reshape x1, local copies, waits for them, and re-layouts, local(): xfour = xconv.reshape(span_count, SEGMENT_LENGTH, head_count, head_size)  13.7 us
  transfers between devices with their start and end apart: 4, of which 1 were waited for; matrix products, arithmetic and copies ran while one was open for 4% of the time, Pallas kernels for 0%

commit v1 on v0

--- a/solution.py
+++ b/solution.py
@@ -83,7 +83,16 @@
     prev_x, prev_bc = passed_along((tail_x, tail_bc), "seq", 1)
     xconv = conv_silu(xin, prev_x, conv_x)
     bc_local = conv_silu(bc_proj, prev_bc, conv_bc)
-    bc_full = lax.all_gather(bc_local, "ch", axis=1, tiled=True)
+    ways = lax.axis_size("ch")
+    up = [(d, (d + 1) % ways) for d in range(ways)]
+    down = [(d, (d - 1) % ways) for d in range(ways)]
+    earlier_2, later = ([bc_local], [bc_local])
+    for _ in range(ways // 2):
+        earlier_2.append(lax.ppermute(earlier_2[-1], "ch", up))
+    for _ in range((ways - 1) // 2):
+        later.append(lax.ppermute(later[-1], "ch", down))
+    line = jnp.concatenate([*earlier_2[::-1], *later[1:]], axis=1)
+    bc_full = jnp.roll(line, (lax.axis_index("ch") - ways // 2) * bc_local.shape[1], axis=1)
     state_size = bc_full.shape[1] // 2
     row_valid = (jnp.arange(row_count) < live_rows).astype(jnp.float32)
     step_size = jax.nn.softplus(dt_raw + dt_bias[None, :]) * row_valid[:, None]

time: 296 us -> 296 us (level)
  blocking collectives: 63.2 us -> 55.8 us
  waiting for transfers between devices: 44.1 us -> 47.3 us
    all_gather x1 -> x0, blocking collectives: 7.2 us -> none  [local(): bc_full = lax.all_gather(bc_local, 'ch', axis=1, tiled=True)]
    unnamed x15 -> x21, local copies, waits for them, and re-layouts: 13 us -> 12.9 us
  transfers between devices with their start and end apart: 4 -> 7, of which waited for: 1 -> 2; matrix products, arithmetic and copies ran while one was open for 4% -> 18% of each run, Pallas kernels for 0% -> 0%
where the time goes in v1:
time: 296 us; the launch traced here: 294 us
  other arithmetic  78.1 us (26%)
  blocking collectives  55.8 us (19%)
  local copies, waits for them, and re-layouts  50.2 us (17%)
  waiting for transfers between devices  47.3 us (16%)
  matrix products  35.5 us (12%)
  starting transfers between devices  26.2 us (9%)
    all_gather x1, blocking collectives, scan_states(): decays = lax.all_gather(factor, axis)  50 us
    all_to_all x1, waiting for transfers between devices, scan_states(): back = lax.all_to_all(jnp.stack(entries, axis=0), axis, 0, 0, tiled=True)  44.7 us
    unnamed x8, other arithmetic  23.8 us
    convert_element_type x1, other arithmetic, local(): return normed.astype(jnp.bfloat16)  23.8 us
    add x1, local copies, waits for them, and re-layouts, local(): intra + inter + skip_gain[None, None, :, None] * xfour.astype(jnp.float32)  19.9 us
    dot_general x1, matrix products, local(): jnp.einsum('chqs,cshp->cqhp', weights, xfour, preferred_element_type=jnp....  16.9 us
    reduce_sum x1, other arithmetic, local(): square_sum = lax.psum(jnp.sum(gated * gated, axis=1), 'ch')  16.2 us
    reshape x1, local copies, waits for them, and re-layouts, local(): xfour = xconv.reshape(span_count, SEGMENT_LENGTH, head_count, head_size)  13.7 us
  transfers between devices with their start and end apart: 7, of which 2 were waited for; matrix products, arithmetic and copies ran while one was open for 18% of the time, Pallas kernels for 0%

profile of v1, /device:TPU:0, one launch (start us, length us, event | category | flops | bytes accessed | tf_op | source)
XLA Modules:
  0.0 294.1 jit_solution(8197544129669939528)
XLA Ops:
  0.7 0.8 constant_dynamic-slice_fusion.2
  1.5 4.9 %collective-permute-start.1 = (bf16[3,64]{0,1:T(8,128)(2,1)S(1)}, bf16[3,64]{0,1:T(8,128)(2,1)S(1)}, u32[]{:S(2)}, u32[]{:S(2)}) collective-permute-start(bf16[3,64]{0,1:T(8,128)(2,1)S(1)} %constant_dynamic-slice_fusion.2), channel_id=1, source_target_pairs={{0,4},{4,8},{8,12},{12,16},{16,20},{20,24},{24,28},{1,5},{5,9},{9,... | collective-permute-start | bytes 1160 | tf_op jit(solution)/shard_map/ppermute | solution.py:14
  6.3 0.9 constant_dynamic-slice_fusion.3
  7.2 3.5 %collective-permute-start = (bf16[3,4096]{1,0:T(4,128)(2,1)S(1)}, bf16[3,4096]{1,0:T(4,128)(2,1)S(1)}, u32[]{:S(2)}, u32[]{:S(2)}) collective-permute-start(bf16[3,4096]{1,0:T(4,128)(2,1)S(1)} %constant_dynamic-slice_fusion.3), channel_id=1, source_target_pairs={{0,4},{4,8},{8,12},{12,16},{16,20},{20,24},{24,28},{1,5},{5,9},{9,... | collective-permute-start | bytes 73736 | tf_op jit(solution)/shard_map/ppermute | solution.py:14
  10.7 1.1 fusion.42
  11.7 0.1 reshape.136
  11.8 0.7 neg.21
  12.5 0.1 multiply_bitcast_fusion
  12.6 0.1 reshape.168
  12.7 2.3 reduce-window.6
  15.0 0.1 slice.183
  15.1 0.1 copy.79
  15.3 0.1 copy_bitcast_fusion
  15.4 0.2 slice_reduce_fusion
  15.6 0.1 copy.85
  15.7 0.1 bitcast_multiply_fusion
  15.8 1.0 slice_convert_fusion.3
  16.8 0.8 bitcast_convert_fusion.3
  17.6 0.0 collective-permute-done.1
  17.6 1.5 multiply_convert_fusion.6
  19.2 0.1 collective-permute-start.2
  19.3 1.7 collective-permute-start.4
  21.1 2.6 collective-permute-done.2
  23.6 0.0 collective-permute-start.3
  23.6 0.0 collective-permute-done
  23.6 18.8 %fusion.26 = bf16[128,8,32,128]{3,1,2,0:T(8,128)(2,1)} fusion(bf16[1024,4096]{1,0:T(8,128)(2,1)} %param.11, f32[4096]{0:T(1024)S(1)} %bitcast.133, bf16[3,4096]{1,0:T(4,128)(2,1)S(1)} %collective-permute-done, f32[4096]{0:T(1024)S(1)} %bitcast.134, f32[4096]{0:T(1024)S(1)} %bitcast.132, f32[4096]{0:T(1024)S(1)} %bitcast.131), kind=kLoop, calls=%fused_computation.37 | loop fusion | flops 104857600 | bytes 16867328
  42.5 9.4 %copy.110 = bf16[128,8,32,128]{3,2,1,0:T(8,128)(2,1)} copy(bf16[128,8,32,128]{3,1,2,0:T(8,128)(2,1)} %fusion.26) | data formatting | bytes 16777216
  51.9 13.7 %copy.83 = bf16[4,256,32,128]{1,3,2,0:T(8,128)(2,1)} copy(bf16[4,256,32,128]{3,2,1,0:T(8,128)(2,1)} %bitcast.118) | data formatting | bytes 16777216 | tf_op jit(solution)/shard_map/reshape | solution.py:99
  65.6 0.0 collective-permute-done.3
  65.6 0.0 collective-permute-done.4
  65.8 0.1 constant_dynamic-slice_fusion
  65.9 0.2 copy.75
  66.1 6.3 %fusion.27 = f32[4,32,128,128]{3,2,1,0:T(8,128)S(1)} fusion(bf16[4,256,128,1]{2,1,3,0:T(8,128)(2,1)S(1)} %bitcast.126, bf16[4,256,32,128]{1,3,2,0:T(8,128)(2,1)} %copy.83, f32[4,256,32]{1,2,0:T(8,128)S(1)} %copy.87), kind=kOutput, calls=%fused_computation.38 | convolution fusion | flops 1086324736 | bytes 17170432 | tf_op jit(solution)/shard_map/csn,cshp->chnp/dot_general | solution.py:116
  72.4 0.6 fusion.53
  73.0 2.6 copy-done
  75.6 2.0 fusion.30
  77.6 4.8 %all-to-all-start = ((f32[8,32,16,128]{3,2,1,0:T(8,128)}), f32[8,32,16,128]{3,2,1,0:T(8,128)S(1)}, u32[]{:S(2)}, u32[]{:S(2)}) async-start(f32[8,32,16,128]{3,2,1,0:T(8,128)} %fusion.30), calls=%async_computation | async-start | bytes 4194304 | tf_op jit(solution)/shard_map/all_to_all | solution.py:35
  82.4 50.0 %all-gather = f32[8,1,32]{2,1,0:T(1,128)S(1)} all-gather(f32[1,1,32]{2,1,0:T(1,128)S(1)} %get-tuple-element.35), channel_id=1, replica_groups=mesh['seq'=8,'ch'=4] {'seq'}, dimensions={0}, use_global_device_ids=true | all-gather | bytes 1152 | tf_op jit(solution)/shard_map/all_gather | solution.py:36
  132.4 0.7 broadcast_dynamic-update-slice_fusion
  133.2 0.0 all-to-all-done
  133.2 0.8 fusion.39
  134.0 0.9 constant_dynamic-update-slice_fusion.12
  134.9 0.8 constant_dynamic-update-slice_fusion.11
  135.7 0.8 constant_dynamic-update-slice_fusion.10
  136.6 0.8 constant_dynamic-update-slice_fusion.9
  137.4 0.8 constant_dynamic-update-slice_fusion.8
  138.2 0.8 fusion.37
  139.0 11.3 %all-to-all-start.1 = ((f32[8,32,16,128]{3,2,1,0:T(8,128)}), f32[8,32,16,128]{3,2,1,0:T(8,128)S(1)}, u32[]{:S(2)}, u32[]{:S(2)}) async-start(f32[8,32,16,128]{3,2,1,0:T(8,128)} %fusion.37), calls=%async_computation.1 | async-start | bytes 4194304 | tf_op jit(solution)/shard_map/all_to_all | solution.py:42
  150.4 0.1 exponential_bitcast_fusion
  150.5 0.2 reshape.134
  150.7 1.3 fusion.34
  152.0 44.7 %all-to-all-done.1 = f32[8,32,16,128]{3,2,1,0:T(8,128)S(1)} async-done(((f32[8,32,16,128]{3,2,1,0:T(8,128)}), f32[8,32,16,128]{3,2,1,0:T(8,128)S(1)}, u32[]{:S(2)}, u32[]{:S(2)}) %all-to-all-start.1) | async-done | bytes 2097184 | tf_op jit(solution)/shard_map/all_to_all | solution.py:42
  196.8 0.3 copy.94
  197.0 0.0 slice-start
  197.0 3.5 %multiply_add_fusion.1 = (f32[1,32,128,128]{3,2,1,0:T(8,128)S(1)}, f32[1,32,128,128]{3,2,1,0:T(8,128)S(1)}, f32[1,32,128,128]{3,2,1,0:T(8,128)S(1)}) fusion(f32[1,32,128,128]{3,2,1,0:T(8,128)S(1)} %bitcast.119, f32[32]{0:T(128)S(1)} %get-tuple-element.6, f32[4,32,128,128]{3,2,1,0:T(8,128)} %copy-done, f32[32]{0:T(128)S(1)} %get-tuple-element.38, ...), kind=kLoop, calls=%fused_computation.48 | loop fusion | flops 5767168 | bytes 14680832 | tf_op jit(solution)/shard_map/add | solution.py:132
  200.6 0.0 slice-start.1
  200.6 0.0 copy-start.3
  200.6 10.9 %fusion.17 = f32[4,256,32,128]{1,3,2,0:T(8,128)} fusion(f32[1,32,128,128]{3,2,1,0:T(8,128)S(1)} %get-tuple-element.14, f32[1,32,128,128]{3,2,1,0:T(8,128)S(1)} %get-tuple-element.13, f32[1,32,128,128]{3,2,1,0:T(8,128)S(1)} %get-tuple-element.15, f32[1,32,128,128]{3,2,1,0:T(8,128)S(1)} %bitcast.120, bf16[4,256,128,1]{1,0,2,3:T(4,128)(2,1)S(1)} %bitcast.130), kind=kOutput, calls=%fused_computation.28 | convolution fusion | flops 6448742400 | bytes 25427968 | tf_op jit(solution)/shard_map/cqn,chnp->cqhp/dot_general | solution.py:137
  211.6 0.0 copy-done.3
  211.6 16.9 %fusion.2 = f32[4,256,32,128]{1,3,2,0:T(8,128)} fusion(bf16[4,256,32,128]{1,3,2,0:T(8,128)(2,1)S(1)} %bitcast.117, f32[4,256,32,128]{1,3,2,0:T(8,128)} %fusion.17, f32[4,32,256]{2,1,0:T(8,128)S(1)} %copy.82, f32[4,32,256]{2,1,0:T(8,128)S(1)} %copy_bitcast_fusion, f32[4,256,256]{2,1,0:T(8,128)S(1)} %copy-done.1, pred[256,256]{1,0:T(8,128)(4,1)S(1)} %iota_compare_fusion, ...), kind=kOutput, calls=%fused_computation.7 | convolution fusion | flops 2218786816 | bytes 43450496 | tf_op jit(solution)/shard_map/chqs,cshp->cqhp/dot_general | solution.py:112
  228.5 19.9 %copy.97 = f32[4,256,32,128]{3,2,1,0:T(8,128)} copy(f32[4,256,32,128]{1,3,2,0:T(8,128)} %fusion.2) | data formatting | bytes 33554432 | tf_op jit(solution)/shard_map/add | solution.py:141
  248.4 16.2 %multiply_reduce_fusion = f32[1024]{0:T(1024)S(1)} fusion(bf16[1024,4096]{1,0:T(8,128)(2,1)} %param.12, f32[128,8,32,128]{3,2,1,0:T(8,128)} %bitcast.114), kind=kLoop, calls=%fused_computation.14 | loop fusion | flops 33553408 | bytes 25169920 | tf_op jit(solution)/shard_map/reduce_sum | solution.py:144
  264.6 5.8 %psum.7 = f32[1024]{0:T(1024)S(1)} all-reduce(f32[1024]{0:T(1024)S(1)} %multiply_reduce_fusion), channel_id=1, replica_groups=mesh['seq'=8,'ch'=4] {'ch'}, use_global_device_ids=true, to_apply=%region_3.4 | all-reduce | flops 1024 | bytes 8192 | tf_op jit(solution)/shard_map/psum | solution.py:144
  270.4 23.8 %multiply_convert_fusion.2 = bf16[1024,4096]{1,0:T(8,128)(2,1)} fusion(f32[1024]{0:T(1024)S(1)} %fusion.46, f32[4096]{0:T(1024)S(1)} %copy-done.2, f32[1024]{0:T(1024)S(1)} %add_rsqrt_fusion, bf16[1024,4096]{1,0:T(8,128)(2,1)} %param.12, f32[128,8,32,128]{3,2,1,0:T(8,128)} %bitcast.115), kind=kLoop, calls=%fused_computation.13 | loop fusion | flops 41943040 | bytes 33579008 | tf_op jit(solution)/shard_map/convert_element_type | solution.py:147
  (29 shorter events, 0.3 us)
Async XLA Ops:
  1.5 16.2 %collective-permute-start.1 = (bf16[3,64]{0,1:T(8,128)(2,1)S(1)}, bf16[3,64]{0,1:T(8,128)(2,1)S(1)}, u32[]{:S(2)}, u32[]{:S(2)}) collective-permute-start(bf16[3,64]{0,1:T(8,128)(2,1)S(1)} %constant_dynamic-slice_fusion.2), channel_id=1, source_target_pairs={{0,4},{4,8},{8,12},{12,16},{16,20},{20,24},{24,28},{1,5},{5,9},{9,... | collective-permute-start | bytes 1160 | tf_op jit(solution)/shard_map/ppermute | solution.py:14
  7.2 16.4 %collective-permute-start = (bf16[3,4096]{1,0:T(4,128)(2,1)S(1)}, bf16[3,4096]{1,0:T(4,128)(2,1)S(1)}, u32[]{:S(2)}, u32[]{:S(2)}) collective-permute-start(bf16[3,4096]{1,0:T(4,128)(2,1)S(1)} %constant_dynamic-slice_fusion.3), channel_id=1, source_target_pairs={{0,4},{4,8},{8,12},{12,16},{16,20},{20,24},{24,28},{1,5},{5,9},{9,... | collective-permute-start | bytes 73736 | tf_op jit(solution)/shard_map/ppermute | solution.py:14
  19.2 4.4 %collective-permute-start.2 = (bf16[1024,64]{0,1:T(8,128)(2,1)S(1)}, bf16[1024,64]{0,1:T(8,128)(2,1)S(1)}, u32[]{:S(2)}, u32[]{:S(2)}) collective-permute-start(bf16[1024,64]{0,1:T(8,128)(2,1)S(1)} %multiply_convert_fusion.6), channel_id=1, source_target_pairs={{0,1},{1,2},{2,3},{3,0},{4,5},{5,6},{6,7},{7,4},{8,9},{9,10},{10,1... | collective-permute-start | bytes 393224 | tf_op jit(solution)/shard_map/ppermute | solution.py:91
  19.3 46.3 %collective-permute-start.4 = (bf16[1024,64]{0,1:T(8,128)(2,1)S(1)}, bf16[1024,64]{0,1:T(8,128)(2,1)S(1)}, u32[]{:S(2)}, u32[]{:S(2)}) collective-permute-start(bf16[1024,64]{0,1:T(8,128)(2,1)S(1)} %multiply_convert_fusion.6), channel_id=1, source_target_pairs={{0,3},{1,0},{2,1},{3,2},{4,7},{5,4},{6,5},{7,6},{8,11},{9,8},{10,9... | collective-permute-start | bytes 393224 | tf_op jit(solution)/shard_map/ppermute | solution.py:93
  23.6 42.0 %collective-permute-start.3 = (bf16[1024,64]{0,1:T(8,128)(2,1)S(1)}, bf16[1024,64]{0,1:T(8,128)(2,1)S(1)}, u32[]{:S(2)}, u32[]{:S(2)}) collective-permute-start(bf16[1024,64]{0,1:T(8,128)(2,1)S(1)} %collective-permute-done.2), channel_id=1, source_target_pairs={{0,1},{1,2},{2,3},{3,0},{4,5},{5,6},{6,7},{7,4},{8,9},{9,10},{10,1... | collective-permute-start | bytes 393224 | tf_op jit(solution)/shard_map/ppermute | solution.py:91
  72.4 3.2 %copy-start = (f32[4,32,128,128]{3,2,1,0:T(8,128)}, f32[4,32,128,128]{3,2,1,0:T(8,128)S(1)}, u32[]{:S(2)}) copy-start(f32[4,32,128,128]{3,2,1,0:T(8,128)S(1)} %fusion.27) | copy-start | bytes 25165828
  77.6 55.6 %all-to-all-start = ((f32[8,32,16,128]{3,2,1,0:T(8,128)}), f32[8,32,16,128]{3,2,1,0:T(8,128)S(1)}, u32[]{:S(2)}, u32[]{:S(2)}) async-start(f32[8,32,16,128]{3,2,1,0:T(8,128)} %fusion.30), calls=%async_computation | async-start | bytes 4194304 | tf_op jit(solution)/shard_map/all_to_all | solution.py:35
  139.0 57.7 %all-to-all-start.1 = ((f32[8,32,16,128]{3,2,1,0:T(8,128)}), f32[8,32,16,128]{3,2,1,0:T(8,128)S(1)}, u32[]{:S(2)}, u32[]{:S(2)}) async-start(f32[8,32,16,128]{3,2,1,0:T(8,128)} %fusion.37), calls=%async_computation.1 | async-start | bytes 4194304 | tf_op jit(solution)/shard_map/all_to_all | solution.py:42
  197.0 14.5 %slice-start = ((s8[8388608]{0:T(1024)(128)(4,1)}), s8[4194304]{0:T(1024)(128)(4,1)S(1)}, s32[]{:S(2)}) async-start(s8[8388608]{0:T(1024)(128)(4,1)} %bitcast.116), calls=%async_computation.2 | async-start | bytes 8388608
  200.6 11.0 %slice-start.1 = ((s8[8388608]{0:T(1024)(128)(4,1)}), s8[4194304]{0:T(1024)(128)(4,1)S(1)}, s32[]{:S(2)}) async-start(s8[8388608]{0:T(1024)(128)(4,1)} %bitcast.116), calls=%async_computation.3 | async-start | bytes 8388608
  200.6 11.0 %copy-start.1 = (f32[4,256,256]{2,1,0:T(8,128)S(1)}, f32[4,256,256]{2,1,0:T(8,128)}, u32[]{:S(2)}) copy-start(f32[4,256,256]{2,1,0:T(8,128)} %fusion.34) | copy-start | bytes 3145732
  200.6 11.0 %copy-start.3 = (f32[32]{0:T(128)S(1)}, f32[32]{0:T(128)}, u32[]{:S(2)}) copy-start(f32[32]{0:T(128)} %param.17) | copy-start | bytes 388
  248.4 22.0 %copy-start.2 = (f32[4096]{0:T(1024)S(1)}, f32[4096]{0:T(1024)}, u32[]{:S(2)}) copy-start(f32[4096]{0:T(1024)} %param.20) | copy-start | bytes 49156
